TPU v7x, 32 devices: a whole 2x2x4 slice. The times are simulated.
32 devices in a mesh: dp: 16 (over z, x, core), group: 2 (over y).
Axes of the slice: x: 2, y: 2, z: 4, core: 2. Of those that a mesh axis runs over, the one named last changes fastest.
Arguments:
- inputs: bfloat16 [32768, 2048], P('dp', 'group'), may hold values from -6 to 6
- grad_out: bfloat16 [32768, 2048], P(('dp', 'group')), may hold values from -0.0625 to 0.0625
- weight: bfloat16 [2048, 2048], P('group'), may hold values from -6 to 6
- old_basis: float32 [2048, 256], P('group'), may hold values from -0.125 to 0.125
- first_moment: float32 [256, 2048], P(None, 'dp'), may hold values from -6 to 6
- second_moment: float32 [256, 2048], P(None, 'dp'), may hold values from 0.1 to 3
Outputs:
- new_weight: bfloat16 [2048, 2048], P('group')
- new_first: float32 [256, 2048], P(None, 'dp')
- new_second: float32 [256, 2048], P(None, 'dp')
- new_basis: float32 [2048, 256], P('group')
All inputs are finite; a program needn't handle non-finite values.
Results may differ from a plain program's by a relative error of at most 0.011.
Values may be sent and summed in bfloat16 or wider, within the bound.
No kernel may reach another device: no remote copies, remote signals or barrier semaphores. Data moves between devices by JAX's collectives and lax.ppermute only.
A program may use at most 64 MiB of HBM per device.

v0:
```python
import jax
import jax.numpy as jnp
from jax import lax
from jax.sharding import PartitionSpec as P

NS_STEPS = 5
STEP = 10
BETA_ONE = 0.9
BETA_TWO = 0.99
ADAM_EPS = 1e-08
HIGHEST = lax.Precision.HIGHEST


def matmul(left, right):
    return jnp.dot(left, right, precision=HIGHEST)


def inner_gram(matrix):
    return lax.dot_general(matrix, matrix, (((0,), (0,)), ((), ())), precision=HIGHEST)


def refine_group(subspace):
    squares = lax.psum(jnp.sum(subspace * subspace), "group")
    iterate = subspace / jnp.sqrt(squares)
    for sweep in range(NS_STEPS):
        gram = lax.psum(inner_gram(iterate).astype(jnp.bfloat16), "group").astype(jnp.float32)
        iterate = 1.5 * iterate - 0.5 * matmul(iterate, gram)
    return iterate


def shards(inputs, grad_out, weight, old_basis, first_moment, second_moment):
    partial_grad = lax.dot_general(
        inputs,
        lax.all_gather(grad_out, "group", axis=0, tiled=True),
        (((0,), (0,)), ((), ())),
        preferred_element_type=jnp.float32,
    )
    grad_block = lax.psum_scatter(partial_grad, "dp", scatter_dimension=1, tiled=True)
    projected = lax.psum(matmul(old_basis.T, grad_block).astype(jnp.bfloat16), "group").astype(
        jnp.float32
    )
    new_first = BETA_ONE * first_moment + (1.0 - BETA_ONE) * projected
    new_second = BETA_TWO * second_moment + (1.0 - BETA_TWO) * projected * projected
    direction = (
        new_first
        / (1.0 - BETA_ONE**STEP)
        / (jnp.sqrt(new_second / (1.0 - BETA_TWO**STEP)) + ADAM_EPS)
    )
    col_count = grad_block.shape[1]
    col_offset = lax.axis_index("dp") * col_count
    own_cols = lax.dynamic_slice_in_dim(weight, col_offset, col_count, 1).astype(jnp.float32)
    updated = (own_cols - matmul(old_basis, direction)).astype(jnp.bfloat16)
    new_weight = lax.all_gather(updated, "dp", axis=1, tiled=True)
    subspace_terms = matmul(grad_block, projected.T)
    subspace = lax.psum(subspace_terms, "dp")
    new_basis = refine_group(subspace)
    return (new_weight, new_first, new_second, new_basis)


def solution(mesh):
    return jax.shard_map(
        shards,
        mesh=mesh,
        in_specs=(
            P("dp", "group"),
            P(("dp", "group"), None),
            P("group", None),
            P("group", None),
            P(None, "dp"),
            P(None, "dp"),
        ),
        out_specs=(P("group", None), P(None, "dp"), P(None, "dp"), P("group", None)),
        check_vma=False,
    )
```

profile of v0, /device:TPU:0, one launch (start us, length us, event | category | flops | bytes accessed | tf_op | source)
XLA Modules:
  0.0 558.3 jit_solution(406713574473706663)
XLA Ops:
  8.0 108.3 %all-gather.3.cloned.1.call-done = bf16[2048,2048]{1,0:T(8,128)(2,1)} async-done(((bf16[1024,2048]{1,0:T(8,128)(2,1)}), bf16[2048,2048]{1,0:T(8,128)(2,1)}) %all-gather.3.cloned.1.call-update) | async-done | bytes 8388624 | tf_op jit(solution)/shard_map/all_gather | solution.py:34
  116.3 14.6 %fusion.21 = f32[1024,2048]{1,0:T(8,128)} fusion(bf16[2048,1024]{1,0:T(8,128)(2,1)} %param.6, bf16[2048,2048]{1,0:T(8,128)(2,1)} %all-gather.3.cloned.1.call-done), kind=kOutput, calls=%fused_computation.38 | convolution fusion | flops 8589934592 | bytes 20971520 | tf_op jit(solution)/shard_map/dot_general | solution.py:32
  130.9 103.7 %reduce-scatter.2.cloned.1.call-done = f32[1024,128]{1,0:T(8,128)} async-done(((f32[1024,2048]{1,0:T(8,128)}), f32[1024,128]{1,0:T(8,128)}) %reduce-scatter.2.cloned.1.call-update) | async-done | bytes 524304 | tf_op jit(solution)/shard_map/reduce_scatter | solution.py:38
  234.6 2.7 fusion.7
  237.4 20.7 %all-reduce.8.cloned.1.call-done = bf16[256,128]{0,1:T(8,128)(2,1)} async-done(((bf16[256,128]{0,1:T(8,128)(2,1)}), bf16[256,128]{0,1:T(8,128)(2,1)}) %all-reduce.8.cloned.1.call-update) | async-done | bytes 65552 | tf_op jit(solution)/shard_map/psum | solution.py:39
  258.1 2.6 fusion.22
  260.8 95.1 %all-reduce.10.cloned.1.call-done = f32[1024,256]{1,0:T(8,128)} async-done(((f32[1024,256]{1,0:T(8,128)}), f32[1024,256]{1,0:T(8,128)}) %all-reduce.10.cloned.1.call-update) | async-done | bytes 1048592 | tf_op jit(solution)/shard_map/psum | solution.py:55
  355.8 2.2 multiply_reduce_fusion
  358.0 5.5 psum.58
  364.3 4.0 convolution_convert_fusion.4
  368.4 20.7 %all-reduce.12.cloned.1.call-done = bf16[256,256]{1,0:T(8,128)(2,1)} async-done(((bf16[256,256]{1,0:T(8,128)(2,1)}), bf16[256,256]{1,0:T(8,128)(2,1)}) %all-reduce.12.cloned.1.call-update) | async-done | bytes 131088 | tf_op jit(solution)/shard_map/psum | solution.py:26
  389.1 1.6 fusion.4
  390.7 2.5 convolution_convert_fusion.3
  393.5 21.4 %all-reduce.14.cloned.1.call-done = bf16[256,256]{1,0:T(8,128)(2,1)} async-done(((bf16[256,256]{1,0:T(8,128)(2,1)}), bf16[256,256]{1,0:T(8,128)(2,1)}) %all-reduce.14.cloned.1.call-update) | async-done | bytes 131088 | tf_op jit(solution)/shard_map/psum | solution.py:26
  414.9 1.5 fusion.3
  416.4 2.5 convolution_convert_fusion.2
  419.0 1.0 constant_dynamic-slice_fusion
  420.0 0.9 copy.16
  421.0 0.8 copy.12
  421.7 18.9 %all-reduce.16.cloned.1.call-done = bf16[256,256]{1,0:T(8,128)(2,1)} async-done(((bf16[256,256]{1,0:T(8,128)(2,1)}), bf16[256,256]{1,0:T(8,128)(2,1)}) %all-reduce.16.cloned.1.call-update) | async-done | bytes 131088 | tf_op jit(solution)/shard_map/psum | solution.py:26
  440.6 1.5 fusion.2
  442.2 2.5 convolution_convert_fusion.1
  444.7 1.0 fusion.8
  445.7 20.6 %all-reduce.18.cloned.1.call-done = bf16[256,256]{1,0:T(8,128)(2,1)} async-done(((bf16[256,256]{1,0:T(8,128)(2,1)}), bf16[256,256]{1,0:T(8,128)(2,1)}) %all-reduce.18.cloned.1.call-update) | async-done | bytes 131088 | tf_op jit(solution)/shard_map/psum | solution.py:26
  466.4 1.5 fusion.1
  467.9 2.5 convolution_convert_fusion
  470.5 2.9 fusion.6
  473.4 0.8 copy.14
  474.9 17.2 %all-reduce.20.cloned.1.call-done = bf16[256,256]{1,0:T(8,128)(2,1)} async-done(((bf16[256,256]{1,0:T(8,128)(2,1)}), bf16[256,256]{1,0:T(8,128)(2,1)}) %all-reduce.20.cloned.1.call-update) | async-done | bytes 131088 | tf_op jit(solution)/shard_map/psum | solution.py:26
  492.1 2.5 fusion
  494.6 50.5 %all-gather.5.cloned.1.call-done = bf16[1024,2048]{0,1:T(8,128)(2,1)} async-done(((bf16[1024,128]{0,1:T(8,128)(2,1)}), bf16[1024,2048]{0,1:T(8,128)(2,1)}) %all-gather.5.cloned.1.call-update) | async-done | bytes 4194320 | tf_op jit(solution)/shard_map/all_gather | solution.py:53
  545.1 6.4 %copy.13 = bf16[1024,2048]{1,0:T(8,128)(2,1)} copy(bf16[1024,2048]{0,1:T(8,128)(2,1)} %all-gather.5.cloned.1.call-done) | data formatting | bytes 8388608
  (30 shorter events, 2.3 us)
Async XLA Ops:
  7.2 227.5 %copy-start = (f32[1024,256]{1,0:T(8,128)S(1)}, f32[1024,256]{1,0:T(8,128)}, u32[]{:S(2)}) copy-start(f32[1024,256]{1,0:T(8,128)} %param.9) | copy-start | bytes 3145732
  7.2 109.1 %all-gather.3.cloned.1.call-start = ((), (), s32[]{:S(2)}) async-start(), calls=%async_computation.1 | async-start | bytes 12582912 | tf_op jit(solution)/shard_map/all_gather | solution.py:34
  7.9 226.7 %reduce-scatter.2.cloned.1.call-start = ((), (), s32[]{:S(2)}) async-start(), calls=%async_computation.2 | async-start | bytes 8912896 | tf_op jit(solution)/shard_map/reduce_scatter | solution.py:38
  130.9 127.2 %all-reduce.8.cloned.1.call-start = ((), (), s32[]{:S(2)}) async-start(), calls=%async_computation.3 | async-start | bytes 131072 | tf_op jit(solution)/shard_map/psum | solution.py:39
  237.4 118.5 %all-reduce.10.cloned.1.call-start = ((), (), s32[]{:S(2)}) async-start(), calls=%async_computation.5 | async-start | bytes 2097152 | tf_op jit(solution)/shard_map/psum | solution.py:55
  260.7 128.4 %all-reduce.12.cloned.1.call-start = ((), (), s32[]{:S(2)}) async-start(), calls=%async_computation.6 | async-start | bytes 262144 | tf_op jit(solution)/shard_map/psum | solution.py:26
  355.8 33.3 %copy-start.1 = (f32[1024,256]{1,0:T(8,128)S(1)}, f32[1024,256]{1,0:T(8,128)}, u32[]{:S(2)}) copy-start(f32[1024,256]{1,0:T(8,128)} %all-reduce.10.cloned.1.call-done) | copy-start | bytes 3145732
  368.3 46.6 %all-reduce.14.cloned.1.call-start = ((), (), s32[]{:S(2)}) async-start(), calls=%async_computation.7 | async-start | bytes 262144 | tf_op jit(solution)/shard_map/psum | solution.py:26
  390.7 30.2 %copy-start.2 = (f32[256,128]{1,0:T(8,128)S(1)}, f32[256,128]{1,0:T(8,128)}, u32[]{:S(2)}) copy-start(f32[256,128]{1,0:T(8,128)} %param.10) | copy-start | bytes 393220
  390.7 30.3 %copy-start.3 = (f32[256,128]{1,0:T(8,128)S(1)}, f32[256,128]{1,0:T(8,128)}, u32[]{:S(2)}) copy-start(f32[256,128]{1,0:T(8,128)} %param.11) | copy-start | bytes 393220
  393.2 47.4 %all-reduce.16.cloned.1.call-start = ((), (), s32[]{:S(2)}) async-start(), calls=%async_computation.8 | async-start | bytes 262144 | tf_op jit(solution)/shard_map/psum | solution.py:26
  419.0 47.4 %all-reduce.18.cloned.1.call-start = ((), (), s32[]{:S(2)}) async-start(), calls=%async_computation.9 | async-start | bytes 262144 | tf_op jit(solution)/shard_map/psum | solution.py:26
  444.7 47.4 %all-reduce.20.cloned.1.call-start = ((), (), s32[]{:S(2)}) async-start(), calls=%async_computation.10 | async-start | bytes 262144 | tf_op jit(solution)/shard_map/psum | solution.py:26
  470.4 74.7 %all-gather.5.cloned.1.call-start = ((), (), s32[]{:S(2)}) async-start(), calls=%async_computation.4 | async-start | bytes 4456448 | tf_op jit(solution)/shard_map/all_gather | solution.py:53
Sparse Core Ops, SparseCore 0:
  9.5 106.6 all-gather.2
  131.0 103.5 reduce-scatter.1
  237.5 20.5 all-reduce.7
  262.0 93.7 all-reduce.9
  368.4 20.6 all-reduce.11
  393.4 21.5 all-reduce.13
  419.1 21.5 all-reduce.15
  444.8 21.5 all-reduce.17
  470.5 21.5 all-reduce.19
  494.7 50.3 all-gather.4
where the time goes:
time: 559 us; the launch traced here: 558 us
  waiting for transfers between devices  478 us (86%)
  matrix products  45.4 us (8%)
  between operations  15 us (3%)
  local copies, waits for them, and re-layouts  10.6 us (2%)
    all_gather x1, waiting for transfers between devices, shards(): lax.all_gather(grad_out, 'group', axis=0, tiled=True)  108 us
    reduce_scatter x1, waiting for transfers between devices, shards(): lax.psum_scatter(partial_grad, 'dp', scatter_dimension=1, tiled=True)  104 us
    psum x5, waiting for transfers between devices, refine_group(): lax.psum(inner_gram(iterate).astype(jnp.bfloat16), 'group')  99 us
    psum x1, waiting for transfers between devices, shards(): subspace = lax.psum(subspace_terms, 'dp')  95.1 us
    all_gather x1, waiting for transfers between devices, shards(): new_weight = lax.all_gather(updated, 'dp', axis=1, tiled=True)  50.5 us
    psum x1, waiting for transfers between devices, shards(): lax.psum(matmul(old_basis.T, grad_block).astype(jnp.bfloat16), 'group')  20.7 us
    dot_general x8, matrix products, matmul(): return jnp.dot(left, right, precision=HIGHEST)  16.8 us
    dot_general x1, matrix products, shards(): lax.dot_general(inputs, lax.all_gather(grad_out, 'group', axis=0, tiled=T...  14.6 us
  transfers between devices with their start and end apart: 10, of which 10 were waited for; matrix products, arithmetic and copies ran while one was open for 2% of the time, Pallas kernels for 0%

commit v1 on v0

--- a/solution.py
+++ b/solution.py
@@ -50,7 +50,8 @@
     col_offset = lax.axis_index("dp") * col_count
     own_cols = lax.dynamic_slice_in_dim(weight, col_offset, col_count, 1).astype(jnp.float32)
     updated = (own_cols - matmul(old_basis, direction)).astype(jnp.bfloat16)
-    new_weight = lax.all_gather(updated, "dp", axis=1, tiled=True)
+    y_new = lax.all_to_all(jnp.stack([updated] * lax.axis_size("dp"), axis=0), "dp", 0, 0)
+    new_weight = jnp.concatenate(y_new, 1)
     subspace_terms = matmul(grad_block, projected.T)
     subspace = lax.psum(subspace_terms, "dp")
     new_basis = refine_group(subspace)

time: 559 us -> 585 us (1.047)
  waiting for transfers between devices: 478 us -> 493 us
  local copies, waits for them, and re-layouts: 10.6 us -> 18.7 us
    psum x1, waiting for transfers between devices: 95.1 us -> 155 us  [shards(): subspace = lax.psum(subspace_terms, 'dp')]
    all_gather x1 -> x0, waiting for transfers between devices: 50.5 us -> none  [shards(): new_weight = lax.all_gather(updated, 'dp', axis=1, tiled=True)]
    psum x5, waiting for transfers between devices: 99 us -> 106 us  [refine_group(): lax.psum(inner_gram(iterate).astype(jnp.bfloat16), 'group')]
    all_to_all x0 -> x1, local copies, waits for them, and re-layouts: none -> 6.44 us  [shards(): lax.all_to_all(jnp.stack([updated] * lax.axis_size('dp'), axis=0), 'dp',...]
  transfers between devices with their start and end apart: 10 -> 10, of which waited for: 10 -> 9; matrix products, arithmetic and copies ran while one was open for 2% -> 5% of each run, Pallas kernels for 0% -> 0%
where the time goes in v1:
time: 585 us; the launch traced here: 584 us
  waiting for transfers between devices  493 us (84%)
  matrix products  42.8 us (7%)
  local copies, waits for them, and re-layouts  18.7 us (3%)
  between operations  14.7 us (3%)
  starting transfers between devices  6.35 us (1%)
    psum x1, waiting for transfers between devices, shards(): subspace = lax.psum(subspace_terms, 'dp')  155 us
    all_gather x1, waiting for transfers between devices, shards(): lax.all_gather(grad_out, 'group', axis=0, tiled=True)  108 us
    psum x5, waiting for transfers between devices, refine_group(): lax.psum(inner_gram(iterate).astype(jnp.bfloat16), 'group')  106 us
    reduce_scatter x1, waiting for transfers between devices, shards(): lax.psum_scatter(partial_grad, 'dp', scatter_dimension=1, tiled=True)  104 us
    psum x1, waiting for transfers between devices, shards(): lax.psum(matmul(old_basis.T, grad_block).astype(jnp.bfloat16), 'group')  19.4 us
    dot_general x1, matrix products, shards(): lax.dot_general(inputs, lax.all_gather(grad_out, 'group', axis=0, tiled=T...  14.7 us
    dot_general x8, matrix products, matmul(): return jnp.dot(left, right, precision=HIGHEST)  14.1 us
    dot_general x5, matrix products, inner_gram(): lax.dot_general(matrix, matrix, (((0,), (0,)), ((), ())), precision=HIGHEST)  14 us
  transfers between devices with their start and end apart: 10, of which 9 were waited for; matrix products, arithmetic and copies ran while one was open for 5% of the time, Pallas kernels for 0%

profile of v1, /device:TPU:0, one launch (start us, length us, event | category | flops | bytes accessed | tf_op | source)
XLA Modules:
  0.0 583.9 jit_solution(16170019780828477489)
XLA Ops:
  8.0 108.3 %all-gather.2.cloned.1.call-done = bf16[2048,2048]{1,0:T(8,128)(2,1)} async-done(((bf16[1024,2048]{1,0:T(8,128)(2,1)}), bf16[2048,2048]{1,0:T(8,128)(2,1)}) %all-gather.2.cloned.1.call-update) | async-done | bytes 8388624 | tf_op jit(solution)/shard_map/all_gather | solution.py:34
  116.3 14.7 %fusion.21 = f32[1024,2048]{1,0:T(8,128)} fusion(bf16[2048,1024]{1,0:T(8,128)(2,1)} %param.6, bf16[2048,2048]{1,0:T(8,128)(2,1)} %all-gather.2.cloned.1.call-done), kind=kOutput, calls=%fused_computation.38 | convolution fusion | flops 8589934592 | bytes 20971520 | tf_op jit(solution)/shard_map/dot_general | solution.py:32
  131.1 103.7 %reduce-scatter.2.cloned.1.call-done = f32[1024,128]{1,0:T(8,128)} async-done(((f32[1024,2048]{1,0:T(8,128)}), f32[1024,128]{1,0:T(8,128)}) %reduce-scatter.2.cloned.1.call-update) | async-done | bytes 524304 | tf_op jit(solution)/shard_map/reduce_scatter | solution.py:38
  234.8 2.7 fusion.7
  237.5 1.0 constant_dynamic-slice_fusion
  238.9 19.4 %all-reduce.8.cloned.1.call-done = bf16[256,128]{0,1:T(8,128)(2,1)} async-done(((bf16[256,128]{0,1:T(8,128)(2,1)}), bf16[256,128]{0,1:T(8,128)(2,1)}) %all-reduce.8.cloned.1.call-update) | async-done | bytes 65552 | tf_op jit(solution)/shard_map/psum | solution.py:39
  258.2 0.9 fusion.8
  259.1 1.2 fusion.6
  260.5 2.8 stack.2
  263.3 5.8 all-to-all-start
  269.2 1.5 fusion.22
  270.8 155.0 %all-reduce.10.cloned.1.call-done = f32[1024,256]{1,0:T(8,128)} async-done(((f32[1024,256]{1,0:T(8,128)}), f32[1024,256]{1,0:T(8,128)}) %all-reduce.10.cloned.1.call-update) | async-done | bytes 1048592 | tf_op jit(solution)/shard_map/psum | solution.py:56
  425.8 2.2 multiply_reduce_fusion
  428.0 5.5 psum.58
  434.2 4.0 convolution_convert_fusion.4
  438.5 20.6 %all-reduce.12.cloned.1.call-done = bf16[256,256]{1,0:T(8,128)(2,1)} async-done(((bf16[256,256]{1,0:T(8,128)(2,1)}), bf16[256,256]{1,0:T(8,128)(2,1)}) %all-reduce.12.cloned.1.call-update) | async-done | bytes 131088 | tf_op jit(solution)/shard_map/psum | solution.py:26
  459.1 1.6 fusion.4
  460.7 2.5 convolution_convert_fusion.3
  463.2 21.6 %all-reduce.14.cloned.1.call-done = bf16[256,256]{1,0:T(8,128)(2,1)} async-done(((bf16[256,256]{1,0:T(8,128)(2,1)}), bf16[256,256]{1,0:T(8,128)(2,1)}) %all-reduce.14.cloned.1.call-update) | async-done | bytes 131088 | tf_op jit(solution)/shard_map/psum | solution.py:26
  484.9 1.5 fusion.3
  486.4 2.5 convolution_convert_fusion.2
  489.0 21.6 %all-reduce.16.cloned.1.call-done = bf16[256,256]{1,0:T(8,128)(2,1)} async-done(((bf16[256,256]{1,0:T(8,128)(2,1)}), bf16[256,256]{1,0:T(8,128)(2,1)}) %all-reduce.16.cloned.1.call-update) | async-done | bytes 131088 | tf_op jit(solution)/shard_map/psum | solution.py:26
  510.6 1.5 fusion.2
  512.1 2.5 convolution_convert_fusion.1
  514.7 21.6 %all-reduce.18.cloned.1.call-done = bf16[256,256]{1,0:T(8,128)(2,1)} async-done(((bf16[256,256]{1,0:T(8,128)(2,1)}), bf16[256,256]{1,0:T(8,128)(2,1)}) %all-reduce.18.cloned.1.call-update) | async-done | bytes 131088 | tf_op jit(solution)/shard_map/psum | solution.py:26
  536.3 1.5 fusion.1
  537.8 2.5 convolution_convert_fusion
  540.4 0.8 copy.28
  541.9 20.2 %all-reduce.20.cloned.1.call-done = bf16[256,256]{1,0:T(8,128)(2,1)} async-done(((bf16[256,256]{1,0:T(8,128)(2,1)}), bf16[256,256]{1,0:T(8,128)(2,1)}) %all-reduce.20.cloned.1.call-update) | async-done | bytes 131088 | tf_op jit(solution)/shard_map/psum | solution.py:26
  562.0 2.5 fusion
  564.5 6.4 %copy.26 = bf16[16,1024,128]{1,2,0:T(8,128)(2,1)} copy(bf16[16,1024,128]{2,1,0:T(8,128)(2,1)} %all-to-all-done) | data formatting | bytes 8388608 | tf_op jit(solution)/shard_map/all_to_all | solution.py:53
  571.0 6.4 %copy.27 = bf16[1024,2048]{1,0:T(8,128)(2,1)} copy(bf16[1024,2048]{0,1:T(8,128)(2,1)} %bitcast.35) | data formatting | bytes 8388608
  (36 shorter events, 2.6 us)
Async XLA Ops:
  7.2 227.6 %copy-start = (f32[1024,256]{1,0:T(8,128)S(1)}, f32[1024,256]{1,0:T(8,128)}, u32[]{:S(2)}) copy-start(f32[1024,256]{1,0:T(8,128)} %param.9) | copy-start | bytes 3145732
  7.2 109.1 %all-gather.2.cloned.1.call-start = ((), (), s32[]{:S(2)}) async-start(), calls=%async_computation.2 | async-start | bytes 12582912 | tf_op jit(solution)/shard_map/all_gather | solution.py:34
  7.9 226.9 %reduce-scatter.2.cloned.1.call-start = ((), (), s32[]{:S(2)}) async-start(), calls=%async_computation.3 | async-start | bytes 8912896 | tf_op jit(solution)/shard_map/reduce_scatter | solution.py:38
  131.0 107.6 %copy-start.4 = (f32[256,128]{1,0:T(8,128)S(1)}, f32[256,128]{1,0:T(8,128)}, u32[]{:S(2)}) copy-start(f32[256,128]{1,0:T(8,128)} %param.10) | copy-start | bytes 393220
  131.0 107.8 %copy-start.5 = (f32[256,128]{1,0:T(8,128)S(1)}, f32[256,128]{1,0:T(8,128)}, u32[]{:S(2)}) copy-start(f32[256,128]{1,0:T(8,128)} %param.11) | copy-start | bytes 393220
  131.0 127.2 %all-reduce.8.cloned.1.call-start = ((), (), s32[]{:S(2)}) async-start(), calls=%async_computation.4 | async-start | bytes 131072 | tf_op jit(solution)/shard_map/psum | solution.py:39
  263.3 5.9 %copy-start.1 = (f32[1024,128]{1,0:T(8,128)S(1)}, f32[1024,128]{1,0:T(8,128)}, u32[]{:S(2)}) copy-start(f32[1024,128]{1,0:T(8,128)} %reduce-scatter.2.cloned.1.call-done) | copy-start | bytes 1572868
  263.3 5.9 %copy-start.3 = (bf16[256,128]{0,1:T(8,128)(2,1)S(1)}, bf16[256,128]{0,1:T(8,128)(2,1)}, u32[]{:S(2)}) copy-start(bf16[256,128]{0,1:T(8,128)(2,1)} %all-reduce.8.cloned.1.call-done) | copy-start | bytes 196612
  263.3 301.2 %all-to-all-start = ((bf16[16,1024,128]{2,1,0:T(8,128)(2,1)}), bf16[16,1024,128]{2,1,0:T(8,128)(2,1)}, u32[]{:S(2)}, u32[]{:S(2)}) async-start(bf16[16,1024,128]{2,1,0:T(8,128)(2,1)} %stack.2), calls=%async_computation.1 | async-start | bytes 8388608 | tf_op jit(solution)/shard_map/all_to_all | solution.py:53
  269.2 156.7 %all-reduce.10.cloned.1.call-start = ((), (), s32[]{:S(2)}) async-start(), calls=%async_computation.5 | async-start | bytes 2097152 | tf_op jit(solution)/shard_map/psum | solution.py:56
  270.8 188.3 %all-reduce.12.cloned.1.call-start = ((), (), s32[]{:S(2)}) async-start(), calls=%async_computation.6 | async-start | bytes 262144 | tf_op jit(solution)/shard_map/psum | solution.py:26
  425.8 33.3 %copy-start.2 = (f32[1024,256]{1,0:T(8,128)S(1)}, f32[1024,256]{1,0:T(8,128)}, u32[]{:S(2)}) copy-start(f32[1024,256]{1,0:T(8,128)} %all-reduce.10.cloned.1.call-done) | copy-start | bytes 3145732
  438.3 46.6 %all-reduce.14.cloned.1.call-start = ((), (), s32[]{:S(2)}) async-start(), calls=%async_computation.7 | async-start | bytes 262144 | tf_op jit(solution)/shard_map/psum | solution.py:26
  463.2 47.4 %all-reduce.16.cloned.1.call-start = ((), (), s32[]{:S(2)}) async-start(), calls=%async_computation.8 | async-start | bytes 262144 | tf_op jit(solution)/shard_map/psum | solution.py:26
  488.9 47.4 %all-reduce.18.cloned.1.call-start = ((), (), s32[]{:S(2)}) async-start(), calls=%async_computation.9 | async-start | bytes 262144 | tf_op jit(solution)/shard_map/psum | solution.py:26
  514.6 47.4 %all-reduce.20.cloned.1.call-start = ((), (), s32[]{:S(2)}) async-start(), calls=%async_computation.10 | async-start | bytes 262144 | tf_op jit(solution)/shard_map/psum | solution.py:26
Sparse Core Ops, SparseCore 0:
  9.5 106.6 all-gather.1
  131.1 103.5 reduce-scatter.1
  237.6 20.5 all-reduce.7
  273.7 152.0 all-reduce.9
  438.4 20.6 all-reduce.11
  463.3 21.5 all-reduce.13
  489.0 21.5 all-reduce.15
  514.8 21.5 all-reduce.17
  540.5 21.5 all-reduce.19
